TPU v7x, 32 devices: a whole 2x2x4 slice. The times are simulated.
32 devices in a mesh: groups: 2 (over y), cols: 4 (over z), slab: 2 (over x), rep: 2 (over core).
Axes of the slice: x: 2, y: 2, z: 4, core: 2. Of those that a mesh axis runs over, the one named last changes fastest.
Arguments:
- fields: bfloat16 [16, 8, 2048, 512], P('cols', 'groups', 'rep', 'slab'), parts along dimension 1, may hold values from -250 to 250
- stresses: bfloat16 [6, 8, 512, 128], P(None, 'groups', 'rep', 'slab'), parts along dimension 1, may hold values from -750 to 750
- planes: int32 [8], P('groups'), parts along dimension 0, may hold values from 0 to 2047, as said below
- active_masks: int32 [3, 6, 256], replicated, may hold values 0 or 1
Outputs:
- coefficients: float32 [3, 12, 256], P(None, 'groups', 'cols'), parts along dimension 1
- misfit: bfloat16 [6, 8, 512, 128], P(None, 'groups', 'rep', 'slab'), parts along dimension 1
There are 2 independent parts, one for each index of `groups`. A program takes and returns all parts, laid end to end along the dimension named above; an argument that names none is the same for every part. Nothing has to cross between parts.
Inputs may be any that keep to these rules, and one draw needn't show every extreme that they name: `planes`: sorted and distinct; either the first is 0 or the last is 2047.
All inputs are finite; a program needn't handle non-finite values.
Results may differ from a plain program's by a relative error of at most 0.0069.
Values may be sent and summed in bfloat16 or wider, within the bound.
No kernel may reach another device: no remote copies, remote signals or barrier semaphores. Data moves between devices by JAX's collectives and lax.ppermute only.
A program may use at most 128 MiB of HBM per device.

v0:
```python
import math
import jax
import jax.numpy as jnp
import numpy as np
from jax import lax
from jax.sharding import PartitionSpec as P

STRESS = 6
TERMS = 256
NY = 2048
PASSES = 3
ITERS = 3
ridge_weight = 0.05
epsilon = 1e-06


def extended(array, sides, width):
    for axis, dim in sides:
        count, length = (lax.axis_size(axis), array.shape[dim])
        up = [(i, (i + 1) % count) for i in range(count)]
        down = [(j, i) for i, j in up]
        last = lax.slice_in_dim(array, length - width, length, axis=dim)
        leading = lax.slice_in_dim(array, 0, width, axis=dim)
        before = lax.ppermute(last, axis, up)
        after = lax.ppermute(leading, axis, down)
        array = jnp.concatenate([before, array, after], axis=dim)
    return array


def tree_sum(value, axes):
    for axis in axes:
        count = lax.axis_size(axis)
        if count & count - 1:
            value = lax.psum(value, axis)
            continue
        step = 1
        while step < count:
            partner = [(i, i ^ step) for i in range(count)]
            value = value + lax.ppermute(value, axis, partner)
            step *= 2
    return value


def kernel(spread):
    offsets = np.arange(13) - 6.0
    values = np.exp(-offsets * offsets / (2.0 * spread * spread))
    return values / values.sum()


def filter_table(cells, first_taps, second_taps, guard, order):
    out_count = cells // 4
    shape = tuple(((cells + 10, 2, out_count)[d] for d in order))
    where = {d: order.index(d) for d in range(3)}
    position = lax.broadcasted_iota(jnp.int32, shape, where[0])
    which = lax.broadcasted_iota(jnp.int32, shape, where[1])
    out_index = lax.broadcasted_iota(jnp.int32, shape, where[2])
    tap_at = position - 1 - 4 * out_index + guard
    table = jnp.zeros(shape, jnp.float32)
    for tap_index in range(13):
        value = jnp.where(
            which == 0, np.float32(first_taps[tap_index]), np.float32(second_taps[tap_index])
        )
        table = jnp.where(tap_at == tap_index, value, table)
    return table


def library(narrow_part, broad_part):
    product = (
        narrow_part.astype(jnp.float32)[:, None, :] * broad_part.astype(jnp.float32)[None, :, :]
    )
    return product.astype(jnp.bfloat16).reshape(
        narrow_part.shape[0] * broad_part.shape[0], narrow_part.shape[1]
    )


def local(fields, stresses, planes, active_masks):
    chan_dev, plane_count, cells_x, cells_z = fields.shape
    coarse_x = cells_x // 4
    coarse_z = cells_z // 4
    row_count = plane_count * coarse_x * coarse_z
    col_devices = lax.axis_size("cols")
    column_index = lax.axis_index("cols")
    term_dev = TERMS // col_devices
    offset = column_index * term_dev
    samples = float(row_count * lax.axis_size("slab") * lax.axis_size("rep"))
    height = 2.0 * (planes.astype(jnp.float32) + 0.5) / NY - 1.0
    root_weight = jnp.sqrt(1.2 - height * height)
    padded = extended(fields, (("slab", 3), ("rep", 2)), 5)
    widened = padded.astype(jnp.float32)
    narrow_taps = kernel(1.5)
    broad_taps = kernel(3.0)
    guard = jnp.minimum(lax.axis_index("rep"), 0)
    span_table = filter_table(cells_z, narrow_taps, broad_taps, guard, (0, 1, 2))
    stream_table = filter_table(cells_x, narrow_taps, broad_taps, guard, (1, 0, 2))
    along_span = jnp.einsum("cpxz,zsn->cpxsn", widened, span_table, precision=lax.Precision.HIGHEST)
    filtered = jnp.einsum(
        "cpxsn,sxm->scpmn", along_span, stream_table, precision=lax.Precision.HIGHEST
    )
    narrow = filtered[0]
    broader = filtered[1]
    narrow_set = narrow.astype(jnp.bfloat16).reshape(chan_dev, row_count)
    broad_set = (
        (broader * root_weight[None, :, None, None])
        .astype(jnp.bfloat16)
        .reshape(chan_dev, row_count)
    )
    weighted = (stresses.astype(jnp.float32) * root_weight[None, :, None, None]).astype(
        jnp.bfloat16
    )
    weighted = weighted.reshape(STRESS, row_count)
    chunk = row_count // col_devices
    block_rows = math.gcd(chunk, 4096)
    block_count = chunk // block_rows
    both_sets = lax.all_to_all(jnp.stack([narrow_set, broad_set]), "cols", 2, 1, tiled=True)
    narrow_all, broad_all = (both_sets[0], both_sets[1])
    weighted = lax.dynamic_slice_in_dim(weighted, column_index * chunk, chunk, 1)

    def gram_step(block_index, carry):
        gram_acc, rhs_acc = carry
        start = block_index * block_rows
        narrow_piece = lax.dynamic_slice_in_dim(narrow_all, start, block_rows, 1)
        broad_piece = lax.dynamic_slice_in_dim(broad_all, start, block_rows, 1)
        all_terms = library(narrow_piece, broad_piece)
        weighted_piece = lax.dynamic_slice_in_dim(weighted, start, block_rows, 1)
        gram_acc = gram_acc + jnp.einsum(
            "ir,jr->ij", all_terms, all_terms, preferred_element_type=jnp.float32
        )
        rhs_acc = rhs_acc + jnp.einsum(
            "ir,kr->ik", all_terms, weighted_piece, preferred_element_type=jnp.float32
        )
        return (gram_acc, rhs_acc)

    gram_part, rhs_part = lax.fori_loop(
        0,
        block_count,
        gram_step,
        (jnp.zeros((TERMS, TERMS), jnp.float32), jnp.zeros((TERMS, STRESS), jnp.float32)),
    )
    full_rows = tree_sum(jnp.concatenate([gram_part, rhs_part], axis=1), ("rep", "slab", "cols"))
    gram_matrix = full_rows[:, :TERMS]
    rhs_sums = full_rows[:, TERMS:]
    column_scale = 1.0 / jnp.sqrt(jnp.diagonal(gram_matrix) / samples + epsilon)
    normal_gram = column_scale[:, None] * gram_matrix * column_scale[None, :] / samples
    target_norm = column_scale[None, :] * rhs_sums.T / samples

    def apply_normal(vector, active):
        product = jnp.einsum(
            "kl,il->ki", active * vector, normal_gram, precision=lax.Precision.HIGHEST
        )
        return active * product + ridge_weight * vector

    def cg_turn(turn_index, state):
        solution_all, remain, direction, norm_now, active = state
        applied = apply_normal(direction, active)
        curve_sum = jnp.sum(direction * applied, axis=1)
        step_size = norm_now / (curve_sum + epsilon)
        solution_all = solution_all + step_size[:, None] * direction
        remain = remain - step_size[:, None] * applied
        norm_next = jnp.sum(remain * remain, axis=1)
        direction = remain + (norm_next / (norm_now + epsilon))[:, None] * direction
        return (solution_all, remain, direction, norm_next, active)

    def cg_pass(pass_index, state):
        solution_all, coefficients = state
        active = lax.dynamic_index_in_dim(active_masks, pass_index, 0, keepdims=False)
        active = active.astype(jnp.float32)
        solution_all = active * solution_all
        remain = active * target_norm - apply_normal(solution_all, active)
        norm_now = jnp.sum(remain * remain, axis=1)
        solution_all = lax.fori_loop(
            0, ITERS, cg_turn, (solution_all, remain, remain, norm_now, active)
        )[0]
        own_part = lax.dynamic_slice_in_dim(solution_all, offset, term_dev, 1)
        coefficients = lax.dynamic_update_index_in_dim(coefficients, own_part, pass_index, 0)
        return (solution_all, coefficients)

    solution_all, coefficients = lax.fori_loop(
        0,
        PASSES,
        cg_pass,
        (
            jnp.zeros((STRESS, TERMS), jnp.float32),
            jnp.zeros((PASSES, STRESS, term_dev), jnp.float32),
        ),
    )
    final_weights = (column_scale[None, :] * solution_all).astype(jnp.bfloat16)

    def misfit_step(block_index, misfit_acc):
        start = block_index * block_rows
        narrow_piece = lax.dynamic_slice_in_dim(narrow_all, start, block_rows, 1)
        broad_piece = lax.dynamic_slice_in_dim(broad_all, start, block_rows, 1)
        all_terms = library(narrow_piece, broad_piece)
        predicted = jnp.dot(final_weights, all_terms, preferred_element_type=jnp.float32)
        weighted_piece = lax.dynamic_slice_in_dim(weighted, start, block_rows, 1)
        piece_misfit = (weighted_piece.astype(jnp.float32) - predicted).astype(jnp.bfloat16)
        return lax.dynamic_update_slice_in_dim(misfit_acc, piece_misfit, start, 1)

    misfit = lax.fori_loop(0, block_count, misfit_step, jnp.zeros((STRESS, chunk), jnp.bfloat16))
    misfit = lax.all_gather(misfit, "cols", axis=1, tiled=True)
    misfit = misfit.reshape(STRESS, plane_count, coarse_x, coarse_z)
    return (coefficients, misfit)


def solution(mesh):
    placed = (
        P("cols", "groups", "rep", "slab"),
        P(None, "groups", "rep", "slab"),
        P("groups"),
        P(),
    )
    return jax.shard_map(
        local,
        mesh=mesh,
        in_specs=placed,
        out_specs=(P(None, "groups", "cols"), P(None, "groups", "rep", "slab")),
        check_vma=False,
    )
```

profile of v0, /device:TPU:0, one launch (start us, length us, event | category | flops | bytes accessed | tf_op | source)
XLA Modules:
  0.0 642.4 jit_solution(13972069590268491912)
XLA Ops:
  0.7 11.6 %copy.29 = bf16[4,4,1024,256]{2,3,1,0:T(8,128)(2,1)} copy(bf16[4,4,1024,256]{3,2,1,0:T(8,128)(2,1)} %param.12) | data formatting | bytes 16777216 | tf_op args[0]
  12.2 1.1 fusion.185
  13.4 3.0 collective-permute-start
  16.9 6.6 %collective-permute-done = bf16[4,4,1024,5]{2,3,1,0:T(8,128)(2,1)S(1)} collective-permute-done((bf16[4,4,1024,5]{2,3,1,0:T(8,128)(2,1)S(1)}, bf16[4,4,1024,5]{2,3,1,0:T(8,128)(2,1)S(1)}, u32[]{:S(2)}, u32[]{:S(2)}) %collective-permute-start) | collective-permute-done | bytes 163872 | tf_op jit(solution)/shard_map/ppermute | solution.py:24
  23.5 4.8 collective-permute-done.1
  28.3 5.5 pad_maximum_fusion
  33.8 3.5 copy-done
  40.6 0.8 copy.41
  41.5 2.3 reshape.115
  45.0 18.4 %concatenate.14 = bf16[4,4,1034,266]{2,3,1,0:T(8,128)(2,1)} concatenate(bf16[4,4,5,266]{2,3,1,0:T(8,128)(2,1)S(1)} %copy.34, bf16[4,4,1024,266]{2,3,1,0:T(8,128)(2,1)} %copy-done, bf16[4,4,5,266]{2,3,1,0:T(8,128)(2,1)S(1)} %copy.35), dimensions={2} | concatenate | bytes 17602816 | tf_op jit(solution)/shard_map/concatenate | solution.py:26
  63.4 10.7 %fusion.10 = f32[4,4,1034,2,64]{2,4,1,0,3:T(8,128)S(1)} fusion(bf16[4,4,1034,266]{2,3,1,0:T(8,128)(2,1)} %concatenate.14, f32[2]{0:T(128)S(1)} %get-tuple-element.567, f32[2]{0:T(128)S(1)} %get-tuple-element.568, f32[2]{0:T(128)S(1)} %get-tuple-element.569, f32[2]{0:T(128)S(1)} %get-tuple-element.570, f32[2]{0:T(128)S(1)} %get-tuple-element.571, ...), kind=kOutput, calls=%fused_computation.32 | convolution fusion | flops 6760434688 | bytes 17273316 | tf_op jit(solution)/shard_map/cpxz,zsn->cpxsn/dot_general | solution.py:95
  74.2 10.1 %fusion.53 = f32[2,4,4,256,64]{3,4,2,1,0:T(8,128)S(1)} fusion(f32[4,4,1034,2,64]{2,4,1,0,3:T(8,128)S(1)} %fusion.10, f32[2]{0:T(128)S(1)} %get-tuple-element.567, f32[2]{0:T(128)S(1)} %get-tuple-element.568, f32[2]{0:T(128)S(1)} %get-tuple-element.569, f32[2]{0:T(128)S(1)} %get-tuple-element.570, f32[2]{0:T(128)S(1)} %get-tuple-element.571, ...), kind=kOutput, calls=%fused_computation.64 | convolution fusion | flops 6520188928 | bytes 10572900 | tf_op jit(solution)/shard_map/cpxsn,sxm->scpmn/dot_general | solution.py:96
  84.4 0.9 slice.62
  85.9 0.9 squeeze.18
  86.7 1.5 copy.36
  88.9 1.2 multiply_convert_fusion.3
  90.9 50.9 %copy.38 = bf16[2,4,65536]{1,0,2:T(2,128)(2,1)} copy(bf16[2,4,65536]{2,1,0:T(4,128)(2,1)S(1)} %pad_maximum_fusion.1) | data formatting | bytes 2097152 | tf_op jit(solution)/shard_map/stack | solution.py:114
  141.8 99.7 %reshape.126 = bf16[4,2,65536]{2,1,0:T(2,128)(2,1)} reshape(bf16[65536,2,4]{2,1,0:T(2,128)(2,1)} %bitcast.80) | data formatting | bytes 2097152
  241.5 5.1 all-to-all-start
  246.6 1.7 constant_dynamic-slice_fusion
  248.3 24.3 %all-to-all-done = bf16[4,2,65536]{2,1,0:T(2,128)(2,1)S(1)} async-done(((bf16[4,2,65536]{2,1,0:T(2,128)(2,1)}), bf16[4,2,65536]{2,1,0:T(2,128)(2,1)S(1)}, u32[]{:S(2)}, u32[]{:S(2)}) %all-to-all-start) | async-done | bytes 1048608 | tf_op jit(solution)/shard_map/all_to_all | solution.py:114
  272.6 85.1 %reshape.127 = bf16[65536,2,4]{2,1,0:T(2,128)(2,1)} reshape(bf16[4,2,65536]{2,1,0:T(2,128)(2,1)S(1)} %all-to-all-done) | data formatting | bytes 2097152
  357.7 62.4 %fusion.183 = (bf16[1,4,4,16384]{2,0,3,1:T(2,128)(2,1)}, bf16[1,4,4,16384]{2,0,3,1:T(2,128)(2,1)}) fusion(bf16[2,4,4,16384]{2,0,3,1:T(2,128)(2,1)} %bitcast.78), kind=kLoop, calls=%fused_computation.197 | loop fusion | bytes 2097152 | tf_op jit(solution)/shard_map/slice | solution.py:115
  420.1 61.1 %copy.39 = bf16[1,4,4,16384]{3,2,1,0:T(4,128)(2,1)S(1)} copy(bf16[1,4,4,16384]{2,0,3,1:T(2,128)(2,1)} %get-tuple-element.562) | data formatting | bytes 1048576 | tf_op jit(solution)/shard_map/slice | solution.py:115
  481.3 61.1 %copy.40 = bf16[1,4,4,16384]{3,2,1,0:T(4,128)(2,1)S(1)} copy(bf16[1,4,4,16384]{2,0,3,1:T(2,128)(2,1)} %get-tuple-element.561) | data formatting | bytes 1048576 | tf_op jit(solution)/shard_map/slice | solution.py:115
  542.5 11.0 %while.79 = (s32[]{:T(128)}, f32[256,256]{1,0:T(8,128)S(1)}, f32[256,6]{0,1:T(8,128)S(1)}, bf16[16,16384]{1,0:T(8,128)(2,1)S(1)}, bf16[16,16384]{1,0:T(8,128)(2,...) while((s32[]{:T(128)}, f32[256,256]{1,0:T(8,128)S(1)}, ...), condition=%wide.region_1.2_spmd.clone, body=%wide.region_0.1_spmd.clone.sunk | while | flops 551816192 | bytes 8204454 | solution.py:133
  544.0 1.5 convolution_add_fusion.5
  546.7 1.5 convolution_add_fusion.5
  549.3 1.5 convolution_add_fusion.5
  552.0 1.5 convolution_add_fusion.5
  553.8 1.7 collective-permute-done.4
  555.5 1.6 collective-permute-start.5
  557.1 9.7 %collective-permute-done.5 = f32[256,262]{1,0:T(8,128)S(1)} collective-permute-done((f32[256,262]{1,0:T(8,128)S(1)}, f32[256,262]{1,0:T(8,128)S(1)}, u32[]{:S(2)}, u32[]{:S(2)}) %collective-permute-start.5) | collective-permute-done | bytes 268320 | tf_op jit(solution)/shard_map/ppermute | solution.py:39
  566.9 10.3 %collective-permute-done.6 = f32[256,262]{1,0:T(8,128)S(1)} collective-permute-done((f32[256,262]{1,0:T(8,128)S(1)}, f32[256,262]{1,0:T(8,128)S(1)}, u32[]{:S(2)}, u32[]{:S(2)}) %collective-permute-start.6) | collective-permute-done | bytes 268320 | tf_op jit(solution)/shard_map/ppermute | solution.py:39
  577.6 18.5 %collective-permute-done.7 = f32[256,262]{1,0:T(8,128)S(1)} collective-permute-done((f32[256,262]{1,0:T(8,128)S(1)}, f32[256,262]{1,0:T(8,128)S(1)}, u32[]{:S(2)}, u32[]{:S(2)}) %collective-permute-start.7) | collective-permute-done | bytes 268320 | tf_op jit(solution)/shard_map/ppermute | solution.py:39
  596.1 2.3 gather_fusion
  598.8 12.1 %while.77 = (s32[]{:T(128)}, f32[6,256]{1,0:T(8,128)S(1)}, f32[3,6,64]{2,1,0:T(8,128)}, s32[3,6,256]{2,1,0:T(8,128)}, f32[6,256]{1,0:T(8,128)S(1)}, /*index=5*/f...) while((s32[]{:T(128)}, f32[6,256]{1,0:T(8,128)S(1)}, f32[3,6,64]{2,1,0:T(8,128)}, ...), condition=%wide.region_8.9_spmd, body=%wide.region_2.8_spmd.sunk | while | flops 9474058 | bytes 660566 | solution.py:177
  599.9 2.2 while.80
  604.0 2.2 while.80
  608.0 2.2 while.80
  610.9 6.4 %while.78 = (s32[]{:T(128)}, bf16[6,16384]{1,0:T(8,128)(2,1)S(1)}, bf16[6,16384]{1,0:T(8,128)(2,1)}, bf16[16,16384]{1,0:T(8,128)(2,1)S(1)}, bf16[16,16384]{1,0:T...) while((s32[]{:T(128)}, bf16[6,16384]{1,0:T(8,128)(2,1)S(1)}, ...), condition=%wide.region_10.11_spmd, body=%wide.region_9.10_spmd.sunk | while | flops 14884870 | bytes 5623963 | solution.py:198
  611.3 1.2 fusion.208
  612.9 1.2 fusion.208
  614.5 1.2 fusion.208
  616.1 1.2 fusion.208
  617.4 21.5 %all_gather.3 = bf16[6,65536]{1,0:T(8,128)(2,1)S(1)} all-gather(bf16[6,16384]{1,0:T(8,128)(2,1)S(1)} %get-tuple-element.439), channel_id=1, replica_groups=mesh['groups'=2,'cols'=4,'slab'=2,'rep'=2] {'cols'}, dimensions={1}, use_global_device_ids=true | all-gather | bytes 983040 | tf_op jit(solution)/shard_map/all_gather | solution.py:199
  638.9 1.6 reshape.116
  640.5 1.4 copy.44
  (140 shorter events, 26.6 us)
Async XLA Ops:
  0.6 15.8 %copy-start.2 = (s32[4]{0:T(128)S(1)}, s32[4]{0:T(128)}, u32[]{:S(2)}) copy-start(s32[4]{0:T(128)} %param.14) | copy-start | bytes 52
  0.6 15.9 %copy-start.1 = (bf16[6,4,256,64]{2,3,1,0:T(8,128)(2,1)S(1)}, bf16[6,4,256,64]{2,3,1,0:T(8,128)(2,1)}, u32[]{:S(2)}) copy-start(bf16[6,4,256,64]{2,3,1,0:T(8,128)(2,1)} %param.13) | copy-start | bytes 2359300
  13.4 10.1 %collective-permute-start = (bf16[4,4,1024,5]{2,3,1,0:T(8,128)(2,1)S(1)}, bf16[4,4,1024,5]{2,3,1,0:T(8,128)(2,1)S(1)}, u32[]{:S(2)}, u32[]{:S(2)}) collective-permute-start(bf16[4,4,1024,5]{2,3,1,0:T(8,128)(2,1)S(1)} %get-tuple-element.565), channel_id=1, source_target_pairs={{0,2},{2,0},{1,3},{3,1},{4,6},{6,4},{5,7},{7,5},{8,10},{10,8},{9,1... | collective-permute-start | bytes 491528 | tf_op jit(solution)/shard_map/ppermute | solution.py:24
  16.4 11.9 %collective-permute-start.1 = (bf16[4,4,1024,5]{2,3,1,0:T(8,128)(2,1)S(1)}, bf16[4,4,1024,5]{2,3,1,0:T(8,128)(2,1)S(1)}, u32[]{:S(2)}, u32[]{:S(2)}) collective-permute-start(bf16[4,4,1024,5]{2,3,1,0:T(8,128)(2,1)S(1)} %get-tuple-element.566), channel_id=1, source_target_pairs={{2,0},{0,2},{3,1},{1,3},{6,4},{4,6},{7,5},{5,7},{10,8},{8,10},{11,... | collective-permute-start | bytes 491528 | tf_op jit(solution)/shard_map/ppermute | solution.py:25
  33.8 3.5 copy-start
  38.5 5.3 collective-permute-start.2
  39.1 5.3 collective-permute-start.3
  241.5 31.1 %all-to-all-start = ((bf16[4,2,65536]{2,1,0:T(2,128)(2,1)}), bf16[4,2,65536]{2,1,0:T(2,128)(2,1)S(1)}, u32[]{:S(2)}, u32[]{:S(2)}) async-start(bf16[4,2,65536]{2,1,0:T(2,128)(2,1)} %reshape.126), calls=%async_computation | async-start | bytes 2097152 | tf_op jit(solution)/shard_map/all_to_all | solution.py:114
  553.7 1.8 collective-permute-start.4
  555.5 11.2 %collective-permute-start.5 = (f32[256,262]{1,0:T(8,128)S(1)}, f32[256,262]{1,0:T(8,128)S(1)}, u32[]{:S(2)}, u32[]{:S(2)}) collective-permute-start(f32[256,262]{1,0:T(8,128)S(1)} %fusion.181), channel_id=1, source_target_pairs={{0,2},{2,0},{1,3},{3,1},{4,6},{6,4},{5,7},{7,5},{8,10},{10,8},{9,1... | collective-permute-start | bytes 804872 | tf_op jit(solution)/shard_map/ppermute | solution.py:39
  566.8 10.4 %collective-permute-start.6 = (f32[256,262]{1,0:T(8,128)S(1)}, f32[256,262]{1,0:T(8,128)S(1)}, u32[]{:S(2)}, u32[]{:S(2)}) collective-permute-start(f32[256,262]{1,0:T(8,128)S(1)} %add.190), channel_id=1, source_target_pairs={{0,4},{4,0},{8,12},{12,8},{1,5},{5,1},{9,13},{13,9},{2,6},{6,2},{1... | collective-permute-start | bytes 804872 | tf_op jit(solution)/shard_map/ppermute | solution.py:39
  577.2 18.8 %collective-permute-start.7 = (f32[256,262]{1,0:T(8,128)S(1)}, f32[256,262]{1,0:T(8,128)S(1)}, u32[]{:S(2)}, u32[]{:S(2)}) collective-permute-start(f32[256,262]{1,0:T(8,128)S(1)} %add.191), channel_id=1, source_target_pairs={{0,8},{4,12},{8,0},{12,4},{1,9},{5,13},{9,1},{13,5},{2,10},{6,14},... | collective-permute-start | bytes 804872 | tf_op jit(solution)/shard_map/ppermute | solution.py:39
where the time goes:
time: 654 us; the launch traced here: 642 us
  local copies, waits for them, and re-layouts  476 us (73%)
  waiting for transfers between devices  75.8 us (12%)
  matrix products  40.1 us (6%)
  blocking collectives  21.5 us (3%)
  other arithmetic  15.8 us (2%)
  starting transfers between devices  10.9 us (2%)
    unnamed x10, local copies, waits for them, and re-layouts  201 us
    slice x3, local copies, waits for them, and re-layouts, local(): narrow_all, broad_all = (both_sets[0], both_sets[1])  185 us
    another operation x1, local copies, waits for them, and re-layouts, local(): jnp.stack([narrow_set, broad_set])  50.9 us
    ppermute x4, waiting for transfers between devices, tree_sum(): value = value + lax.ppermute(value, axis, partner)  40.1 us
    all_to_all x1, waiting for transfers between devices, local(): lax.all_to_all(jnp.stack([narrow_set, broad_set]), 'cols', 2, 1, tiled=True)  24.3 us
    all_gather x1, blocking collectives, local(): misfit = lax.all_gather(misfit, 'cols', axis=1, tiled=True)  21.5 us
    concatenate x1, local copies, waits for them, and re-layouts, extended(): array = jnp.concatenate([before, array, after], axis=dim)  18.4 us
  transfers between devices with their start and end apart: 9, of which 7 were waited for; matrix products, arithmetic and copies ran while one was open for 1% of the time, Pallas kernels for 0%

commit v1 on v0

--- a/solution.py
+++ b/solution.py
@@ -111,7 +111,21 @@
     chunk = row_count // col_devices
     block_rows = math.gcd(chunk, 4096)
     block_count = chunk // block_rows
-    both_sets = lax.all_to_all(jnp.stack([narrow_set, broad_set]), "cols", 2, 1, tiled=True)
+    x = jnp.stack([narrow_set, broad_set])
+    ways, here = (lax.axis_size("cols"), lax.axis_index("cols"))
+    width_2 = x.shape[2] // ways
+    dims = list(x.shape)
+    dims[2] = width_2
+    height_2 = dims[1]
+    dims[1] = height_2 * ways
+    both_sets = jnp.zeros(dims, x.dtype)
+    for mask in range(ways):
+        part = lax.dynamic_slice_in_dim(x, (here ^ mask) * width_2, width_2, axis=2)
+        if mask:
+            part = lax.ppermute(part, "cols", [(d_2, d_2 ^ mask) for d_2 in range(ways)])
+        both_sets = lax.dynamic_update_slice_in_dim(
+            both_sets, part, (here ^ mask) * height_2, axis=1
+        )
     narrow_all, broad_all = (both_sets[0], both_sets[1])
     weighted = lax.dynamic_slice_in_dim(weighted, column_index * chunk, chunk, 1)
 

time: 654 us -> 219 us (0.33); the launches traced: 642 us -> 217 us
  local copies, waits for them, and re-layouts: 476 us -> 55.6 us
  waiting for transfers between devices: 75.8 us -> 66.2 us
  starting transfers between devices: 10.9 us -> 17.5 us
    unnamed x10 -> x8, local copies, waits for them, and re-layouts: 201 us -> 16.5 us
    slice x3 -> x0, local copies, waits for them, and re-layouts: 185 us -> none  [local(): narrow_all, broad_all = (both_sets[0], both_sets[1])]
    another operation x1 -> x0, local copies, waits for them, and re-layouts: 50.9 us -> none  [local(): jnp.stack([narrow_set, broad_set])]
    all_to_all x1 -> x0, waiting for transfers between devices: 24.3 us -> none  [local(): lax.all_to_all(jnp.stack([narrow_set, broad_set]), 'cols', 2, 1, tiled=True)]
    ppermute x0 -> x3, waiting for transfers between devices: none -> 18.6 us  [local(): lax.ppermute(part, 'cols', [(d_2, d_2 ^ mask) for d_2 in range(ways)])]
    ppermute x4, starting transfers between devices: 2.04 us -> 9.32 us  [tree_sum(): value = value + lax.ppermute(value, axis, partner)]
  transfers between devices with their start and end apart: 9 -> 11, of which waited for: 7 -> 8; matrix products, arithmetic and copies ran while one was open for 1% -> 3% of each run, Pallas kernels for 0% -> 0%
where the time goes in v1:
time: 219 us; the launch traced here: 217 us
  waiting for transfers between devices  66.2 us (30%)
  local copies, waits for them, and re-layouts  55.6 us (25%)
  matrix products  40 us (18%)
  blocking collectives  21.7 us (10%)
  starting transfers between devices  17.5 us (8%)
  other arithmetic  15 us (7%)
    ppermute x4, waiting for transfers between devices, tree_sum(): value = value + lax.ppermute(value, axis, partner)  36.2 us
    all_gather x1, blocking collectives, local(): misfit = lax.all_gather(misfit, 'cols', axis=1, tiled=True)  21.7 us
    ppermute x3, waiting for transfers between devices, local(): lax.ppermute(part, 'cols', [(d_2, d_2 ^ mask) for d_2 in range(ways)])  18.6 us
    concatenate x1, local copies, waits for them, and re-layouts, extended(): array = jnp.concatenate([before, array, after], axis=dim)  18.4 us
    unnamed x8, local copies, waits for them, and re-layouts  16.5 us
    dot_general x1, matrix products, local(): jnp.einsum('cpxz,zsn->cpxsn', widened, span_table, precision=lax.Precisio...  10.7 us
    dot_general x1, matrix products, local(): jnp.einsum('cpxsn,sxm->scpmn', along_span, stream_table, precision=lax.Pr...  10.1 us
    ppermute x4, starting transfers between devices, tree_sum(): value = value + lax.ppermute(value, axis, partner)  9.32 us
  transfers between devices with their start and end apart: 11, of which 8 were waited for; matrix products, arithmetic and copies ran while one was open for 3% of the time, Pallas kernels for 0%

profile of v1, /device:TPU:0, one launch (start us, length us, event | category | flops | bytes accessed | tf_op | source)
XLA Modules:
  0.0 217.4 jit_solution(6348570329536142480)
XLA Ops:
  0.7 11.6 %copy.24 = bf16[4,4,1024,256]{2,3,1,0:T(8,128)(2,1)} copy(bf16[4,4,1024,256]{3,2,1,0:T(8,128)(2,1)} %param.12) | data formatting | bytes 16777216 | tf_op args[0]
  12.2 1.1 fusion.189
  13.4 3.0 %collective-permute-start = (bf16[4,4,1024,5]{2,3,1,0:T(8,128)(2,1)S(1)}, bf16[4,4,1024,5]{2,3,1,0:T(8,128)(2,1)S(1)}, u32[]{:S(2)}, u32[]{:S(2)}) collective-permute-start(bf16[4,4,1024,5]{2,3,1,0:T(8,128)(2,1)S(1)} %get-tuple-element.563), channel_id=1, source_target_pairs={{0,2},{2,0},{1,3},{3,1},{4,6},{6,4},{5,7},{7,5},{8,10},{10,8},{9,1... | collective-permute-start | bytes 491528 | tf_op jit(solution)/shard_map/ppermute | solution.py:24
  16.9 6.6 %collective-permute-done = bf16[4,4,1024,5]{2,3,1,0:T(8,128)(2,1)S(1)} collective-permute-done((bf16[4,4,1024,5]{2,3,1,0:T(8,128)(2,1)S(1)}, bf16[4,4,1024,5]{2,3,1,0:T(8,128)(2,1)S(1)}, u32[]{:S(2)}, u32[]{:S(2)}) %collective-permute-start) | collective-permute-done | bytes 163872 | tf_op jit(solution)/shard_map/ppermute | solution.py:24
  23.5 4.8 %collective-permute-done.1 = bf16[4,4,1024,5]{2,3,1,0:T(8,128)(2,1)S(1)} collective-permute-done((bf16[4,4,1024,5]{2,3,1,0:T(8,128)(2,1)S(1)}, bf16[4,4,1024,5]{2,3,1,0:T(8,128)(2,1)S(1)}, u32[]{:S(2)}, u32[]{:S(2)}) %collective-permute-start.1) | collective-permute-done | bytes 163872 | tf_op jit(solution)/shard_map/ppermute | solution.py:25
  28.3 5.5 %pad_maximum_fusion = bf16[4,4,1024,266]{2,3,1,0:T(8,128)(2,1)S(1)} fusion(bf16[4,4,1024,5]{2,3,1,0:T(8,128)(2,1)S(1)} %collective-permute-done.1, bf16[4,4,1024,256]{2,3,1,0:T(8,128)(2,1)} %copy.24, bf16[4,4,1024,5]{2,3,1,0:T(8,128)(2,1)S(1)} %collective-permute-done), kind=kLoop, calls=%fused_computation.34 | loop fusion | flops 26148864 | bytes 17432576 | tf_op jit(solution)/shard_map/concatenate | solution.py:26
  33.8 3.5 %copy-done = bf16[4,4,1024,266]{2,3,1,0:T(8,128)(2,1)} copy-done((bf16[4,4,1024,266]{2,3,1,0:T(8,128)(2,1)}, bf16[4,4,1024,266]{2,3,1,0:T(8,128)(2,1)S(1)}, u32[]{:S(2)}) %copy-start) | copy-done | bytes 8716312
  39.9 0.9 copy.33
  40.8 2.3 %reshape.111 = bf16[6,65536]{1,0:T(8,128)(2,1)} reshape(bf16[6,4,256,64]{3,2,1,0:T(8,128)(2,1)S(1)} %copy.33) | data formatting | bytes 1572864 | tf_op jit(solution)/shard_map/reshape | solution.py:110
  44.3 18.4 %concatenate.14 = bf16[4,4,1034,266]{2,3,1,0:T(8,128)(2,1)} concatenate(bf16[4,4,5,266]{2,3,1,0:T(8,128)(2,1)S(1)} %copy.29, bf16[4,4,1024,266]{2,3,1,0:T(8,128)(2,1)} %copy-done, bf16[4,4,5,266]{2,3,1,0:T(8,128)(2,1)S(1)} %copy.30), dimensions={2} | concatenate | bytes 17602816 | tf_op jit(solution)/shard_map/concatenate | solution.py:26
  62.7 10.7 %fusion.10 = f32[4,4,1034,2,64]{2,4,1,0,3:T(8,128)S(1)} fusion(bf16[4,4,1034,266]{2,3,1,0:T(8,128)(2,1)} %concatenate.14, f32[2]{0:T(128)S(1)} %get-tuple-element.571, f32[2]{0:T(128)S(1)} %get-tuple-element.572, f32[2]{0:T(128)S(1)} %get-tuple-element.573, f32[2]{0:T(128)S(1)} %get-tuple-element.574, f32[2]{0:T(128)S(1)} %get-tuple-element.575, ...), kind=kOutput, calls=%fused_computation.32 | convolution fusion | flops 6760434688 | bytes 17273316 | tf_op jit(solution)/shard_map/cpxz,zsn->cpxsn/dot_general | solution.py:95
  73.4 10.1 %fusion.53 = f32[2,4,4,256,64]{3,4,2,1,0:T(8,128)S(1)} fusion(f32[4,4,1034,2,64]{2,4,1,0,3:T(8,128)S(1)} %fusion.10, f32[2]{0:T(128)S(1)} %get-tuple-element.571, f32[2]{0:T(128)S(1)} %get-tuple-element.572, f32[2]{0:T(128)S(1)} %get-tuple-element.573, f32[2]{0:T(128)S(1)} %get-tuple-element.574, f32[2]{0:T(128)S(1)} %get-tuple-element.575, ...), kind=kOutput, calls=%fused_computation.64 | convolution fusion | flops 6520188928 | bytes 10572900 | tf_op jit(solution)/shard_map/cpxsn,sxm->scpmn/dot_general | solution.py:96
  83.6 0.9 slice.62
  85.1 0.9 squeeze.18
  85.9 1.5 copy.31
  88.5 0.9 fusion.80
  89.4 1.9 collective-permute-start.4
  91.3 1.7 constant_dynamic-slice_fusion
  92.9 2.6 %collective-permute-start.5 = (bf16[2,4,16384]{2,1,0:T(4,128)(2,1)S(1)}, bf16[2,4,16384]{2,1,0:T(4,128)(2,1)S(1)}, u32[]{:S(2)}, u32[]{:S(2)}) collective-permute-start(bf16[2,4,16384]{2,1,0:T(4,128)(2,1)S(1)} %get-tuple-element.570), channel_id=1, source_target_pairs={{0,8},{4,12},{8,0},{12,4},{1,9},{5,13},{9,1},{13,5},{2,10},{6,14},... | collective-permute-start | bytes 786440 | tf_op jit(solution)/shard_map/ppermute | solution.py:125
  95.5 6.1 %collective-permute-done.4 = bf16[2,4,16384]{2,1,0:T(4,128)(2,1)S(1)} collective-permute-done((bf16[2,4,16384]{2,1,0:T(4,128)(2,1)S(1)}, bf16[2,4,16384]{2,1,0:T(4,128)(2,1)S(1)}, u32[]{:S(2)}, u32[]{:S(2)}) %collective-permute-start.4) | collective-permute-done | bytes 262176 | tf_op jit(solution)/shard_map/ppermute | solution.py:125
  101.8 12.5 %collective-permute-done.5 = bf16[2,4,16384]{2,1,0:T(4,128)(2,1)S(1)} collective-permute-done((bf16[2,4,16384]{2,1,0:T(4,128)(2,1)S(1)}, bf16[2,4,16384]{2,1,0:T(4,128)(2,1)S(1)}, u32[]{:S(2)}, u32[]{:S(2)}) %collective-permute-start.5) | collective-permute-done | bytes 262176 | tf_op jit(solution)/shard_map/ppermute | solution.py:125
  114.8 10.7 %while.79 = (s32[]{:T(128)}, f32[256,256]{1,0:T(8,128)S(1)}, f32[256,6]{0,1:T(8,128)S(1)}, bf16[16,16384]{1,0:T(8,128)(2,1)S(1)}, bf16[16,16384]{1,0:T(8,128)(2,...) while((s32[]{:T(128)}, f32[256,256]{1,0:T(8,128)S(1)}, ...), condition=%wide.region_1.2_spmd.clone, body=%wide.region_0.1_spmd.clone.sunk | while | flops 551816192 | bytes 8204454 | solution.py:147
  115.2 0.8 convolution_add_fusion.4
  116.0 1.5 convolution_add_fusion.5
  118.6 1.5 convolution_add_fusion.5
  120.5 0.8 convolution_add_fusion.4
  121.3 1.5 convolution_add_fusion.5
  124.0 1.5 convolution_add_fusion.5
  125.7 1.7 collective-permute-done.7
  127.5 1.6 collective-permute-start.8
  129.1 9.7 %collective-permute-done.8 = f32[256,262]{1,0:T(8,128)S(1)} collective-permute-done((f32[256,262]{1,0:T(8,128)S(1)}, f32[256,262]{1,0:T(8,128)S(1)}, u32[]{:S(2)}, u32[]{:S(2)}) %collective-permute-start.8) | collective-permute-done | bytes 268320 | tf_op jit(solution)/shard_map/ppermute | solution.py:39
  138.8 4.8 %collective-permute-start.9 = (f32[256,262]{1,0:T(8,128)S(1)}, f32[256,262]{1,0:T(8,128)S(1)}, u32[]{:S(2)}, u32[]{:S(2)}) collective-permute-start(f32[256,262]{1,0:T(8,128)S(1)} %add.219), channel_id=1, source_target_pairs={{0,4},{4,0},{8,12},{12,8},{1,5},{5,1},{9,13},{13,9},{2,6},{6,2},{1... | collective-permute-start | bytes 804872 | tf_op jit(solution)/shard_map/ppermute | solution.py:39
  143.6 8.6 %collective-permute-done.9 = f32[256,262]{1,0:T(8,128)S(1)} collective-permute-done((f32[256,262]{1,0:T(8,128)S(1)}, f32[256,262]{1,0:T(8,128)S(1)}, u32[]{:S(2)}, u32[]{:S(2)}) %collective-permute-start.9) | collective-permute-done | bytes 268320 | tf_op jit(solution)/shard_map/ppermute | solution.py:39
  152.2 2.8 %collective-permute-start.10 = (f32[256,262]{1,0:T(8,128)S(1)}, f32[256,262]{1,0:T(8,128)S(1)}, u32[]{:S(2)}, u32[]{:S(2)}) collective-permute-start(f32[256,262]{1,0:T(8,128)S(1)} %add.220), channel_id=1, source_target_pairs={{0,8},{4,12},{8,0},{12,4},{1,9},{5,13},{9,1},{13,5},{2,10},{6,14},... | collective-permute-start | bytes 804872 | tf_op jit(solution)/shard_map/ppermute | solution.py:39
  155.1 16.2 %collective-permute-done.10 = f32[256,262]{1,0:T(8,128)S(1)} collective-permute-done((f32[256,262]{1,0:T(8,128)S(1)}, f32[256,262]{1,0:T(8,128)S(1)}, u32[]{:S(2)}, u32[]{:S(2)}) %collective-permute-start.10) | collective-permute-done | bytes 268320 | tf_op jit(solution)/shard_map/ppermute | solution.py:39
  171.4 2.3 %gather_fusion = f32[256]{0:T(256)S(1)} fusion(f32[256,256]{1,0:T(8,128)S(1)} %slice.51, s32[256]{0:T(256)S(1)} %bitcast.78), kind=kCustom, calls=%fused_computation | custom fusion | bytes 4096 | tf_op jit(solution)/shard_map/jit(diagonal)/cond/branch_0_fun/gather | solution.py:156
  174.1 12.1 %while.77 = (s32[]{:T(128)}, f32[6,256]{1,0:T(8,128)S(1)}, f32[3,6,64]{2,1,0:T(8,128)}, s32[3,6,256]{2,1,0:T(8,128)}, f32[6,256]{1,0:T(8,128)S(1)}, /*index=5*/f...) while((s32[]{:T(128)}, f32[6,256]{1,0:T(8,128)S(1)}, f32[3,6,64]{2,1,0:T(8,128)}, ...), condition=%wide.region_8.9_spmd, body=%wide.region_2.8_spmd.sunk | while | flops 9474058 | bytes 660566 | solution.py:191
  175.2 2.2 %while.80 = (s32[]{:T(128)}, f32[6,256]{1,0:T(8,128)S(1)}, f32[6,256]{1,0:T(8,128)S(1)}, f32[6,256]{1,0:T(8,128)S(1)}, f32[6]{0:T(128)S(1)}, /*index=5*/f32[6,256]{1,0:T(8,128)S(1)}, f32[256,256]{1,0:T(8,128)S(1)}, s32[]{:T(128)}) while((s32[]{:T(128)}, f32[6,256]{1,0:T(8,128)S(1)}, f32[6,256]{1,0:T(8,128)S(1)}, f32[6,256]{1,0:T(8,128)S(1)}, ...), condition=%wide.region_7.7_spmd, body=%wide.region_4.6_spmd.sunk | while | flops 4740110 | bytes 330125 | solution.py:184
  179.2 2.2 %while.80 = (s32[]{:T(128)}, f32[6,256]{1,0:T(8,128)S(1)}, f32[6,256]{1,0:T(8,128)S(1)}, f32[6,256]{1,0:T(8,128)S(1)}, f32[6]{0:T(128)S(1)}, /*index=5*/f32[6,256]{1,0:T(8,128)S(1)}, f32[256,256]{1,0:T(8,128)S(1)}, s32[]{:T(128)}) while((s32[]{:T(128)}, f32[6,256]{1,0:T(8,128)S(1)}, f32[6,256]{1,0:T(8,128)S(1)}, f32[6,256]{1,0:T(8,128)S(1)}, ...), condition=%wide.region_7.7_spmd, body=%wide.region_4.6_spmd.sunk | while | flops 4740110 | bytes 330125 | solution.py:184
  183.3 2.2 %while.80 = (s32[]{:T(128)}, f32[6,256]{1,0:T(8,128)S(1)}, f32[6,256]{1,0:T(8,128)S(1)}, f32[6,256]{1,0:T(8,128)S(1)}, f32[6]{0:T(128)S(1)}, /*index=5*/f32[6,256]{1,0:T(8,128)S(1)}, f32[256,256]{1,0:T(8,128)S(1)}, s32[]{:T(128)}) while((s32[]{:T(128)}, f32[6,256]{1,0:T(8,128)S(1)}, f32[6,256]{1,0:T(8,128)S(1)}, f32[6,256]{1,0:T(8,128)S(1)}, ...), condition=%wide.region_7.7_spmd, body=%wide.region_4.6_spmd.sunk | while | flops 4740110 | bytes 330125 | solution.py:184
  186.2 6.4 %while.78 = (s32[]{:T(128)}, bf16[6,16384]{1,0:T(8,128)(2,1)S(1)}, bf16[6,16384]{1,0:T(8,128)(2,1)}, bf16[16,16384]{1,0:T(8,128)(2,1)S(1)}, bf16[16,16384]{1,0:T...) while((s32[]{:T(128)}, bf16[6,16384]{1,0:T(8,128)(2,1)S(1)}, ...), condition=%wide.region_10.11_spmd, body=%wide.region_9.10_spmd.sunk | while | flops 14884870 | bytes 5623963 | solution.py:212
  186.6 1.2 fusion.212
  188.2 1.2 fusion.212
  189.8 1.2 fusion.212
  191.4 1.2 fusion.212
  192.6 21.7 %all_gather.3 = bf16[6,65536]{1,0:T(8,128)(2,1)S(1)} all-gather(bf16[6,16384]{1,0:T(8,128)(2,1)S(1)} %get-tuple-element.439), channel_id=1, replica_groups=mesh['groups'=2,'cols'=4,'slab'=2,'rep'=2] {'cols'}, dimensions={1}, use_global_device_ids=true | all-gather | bytes 983040 | tf_op jit(solution)/shard_map/all_gather | solution.py:213
  214.4 1.6 reshape.112
  216.0 1.4 copy.36
  (141 shorter events, 23.8 us)
Async XLA Ops:
  0.6 15.8 %copy-start.2 = (s32[4]{0:T(128)S(1)}, s32[4]{0:T(128)}, u32[]{:S(2)}) copy-start(s32[4]{0:T(128)} %param.14) | copy-start | bytes 52
  0.6 15.9 %copy-start.1 = (bf16[6,4,256,64]{2,3,1,0:T(8,128)(2,1)S(1)}, bf16[6,4,256,64]{2,3,1,0:T(8,128)(2,1)}, u32[]{:S(2)}) copy-start(bf16[6,4,256,64]{2,3,1,0:T(8,128)(2,1)} %param.13) | copy-start | bytes 2359300
  13.4 10.1 %collective-permute-start = (bf16[4,4,1024,5]{2,3,1,0:T(8,128)(2,1)S(1)}, bf16[4,4,1024,5]{2,3,1,0:T(8,128)(2,1)S(1)}, u32[]{:S(2)}, u32[]{:S(2)}) collective-permute-start(bf16[4,4,1024,5]{2,3,1,0:T(8,128)(2,1)S(1)} %get-tuple-element.563), channel_id=1, source_target_pairs={{0,2},{2,0},{1,3},{3,1},{4,6},{6,4},{5,7},{7,5},{8,10},{10,8},{9,1... | collective-permute-start | bytes 491528 | tf_op jit(solution)/shard_map/ppermute | solution.py:24
  16.4 11.9 %collective-permute-start.1 = (bf16[4,4,1024,5]{2,3,1,0:T(8,128)(2,1)S(1)}, bf16[4,4,1024,5]{2,3,1,0:T(8,128)(2,1)S(1)}, u32[]{:S(2)}, u32[]{:S(2)}) collective-permute-start(bf16[4,4,1024,5]{2,3,1,0:T(8,128)(2,1)S(1)} %get-tuple-element.564), channel_id=1, source_target_pairs={{2,0},{0,2},{3,1},{1,3},{6,4},{4,6},{7,5},{5,7},{10,8},{8,10},{11,... | collective-permute-start | bytes 491528 | tf_op jit(solution)/shard_map/ppermute | solution.py:25
  33.8 3.5 %copy-start = (bf16[4,4,1024,266]{2,3,1,0:T(8,128)(2,1)}, bf16[4,4,1024,266]{2,3,1,0:T(8,128)(2,1)S(1)}, u32[]{:S(2)}) copy-start(bf16[4,4,1024,266]{2,3,1,0:T(8,128)(2,1)S(1)} %pad_maximum_fusion) | copy-start | bytes 26148868
  38.5 4.6 %collective-permute-start.2 = (bf16[4,4,5,266]{3,1,2,0:T(4,128)(2,1)S(1)}, bf16[4,4,5,266]{3,1,2,0:T(4,128)(2,1)S(1)}, u32[]{:S(2)}, u32[]{:S(2)}) collective-permute-start(bf16[4,4,5,266]{3,1,2,0:T(4,128)(2,1)S(1)} %copy.27), channel_id=1, source_target_pairs={{0,1},{1,0},{2,3},{3,2},{4,5},{5,4},{6,7},{7,6},{8,9},{9,8},{10,11... | collective-permute-start | bytes 127688 | tf_op jit(solution)/shard_map/ppermute | solution.py:24
  39.1 4.6 %collective-permute-start.3 = (bf16[4,4,5,266]{3,1,2,0:T(4,128)(2,1)S(1)}, bf16[4,4,5,266]{3,1,2,0:T(4,128)(2,1)S(1)}, u32[]{:S(2)}, u32[]{:S(2)}) collective-permute-start(bf16[4,4,5,266]{3,1,2,0:T(4,128)(2,1)S(1)} %copy.28), channel_id=1, source_target_pairs={{1,0},{0,1},{3,2},{2,3},{5,4},{4,5},{7,6},{6,7},{9,8},{8,9},{11,10... | collective-permute-start | bytes 127688 | tf_op jit(solution)/shard_map/ppermute | solution.py:25
  89.4 12.2 %collective-permute-start.4 = (bf16[2,4,16384]{2,1,0:T(4,128)(2,1)S(1)}, bf16[2,4,16384]{2,1,0:T(4,128)(2,1)S(1)}, u32[]{:S(2)}, u32[]{:S(2)}) collective-permute-start(bf16[2,4,16384]{2,1,0:T(4,128)(2,1)S(1)} %get-tuple-element.569), channel_id=1, source_target_pairs={{0,4},{4,0},{8,12},{12,8},{1,5},{5,1},{9,13},{13,9},{2,6},{6,2},{1... | collective-permute-start | bytes 786440 | tf_op jit(solution)/shard_map/ppermute | solution.py:125
  92.9 21.3 %collective-permute-start.5 = (bf16[2,4,16384]{2,1,0:T(4,128)(2,1)S(1)}, bf16[2,4,16384]{2,1,0:T(4,128)(2,1)S(1)}, u32[]{:S(2)}, u32[]{:S(2)}) collective-permute-start(bf16[2,4,16384]{2,1,0:T(4,128)(2,1)S(1)} %get-tuple-element.570), channel_id=1, source_target_pairs={{0,8},{4,12},{8,0},{12,4},{1,9},{5,13},{9,1},{13,5},{2,10},{6,14},... | collective-permute-start | bytes 786440 | tf_op jit(solution)/shard_map/ppermute | solution.py:125
  95.5 18.9 %collective-permute-start.6 = (bf16[2,4,16384]{2,1,0:T(4,128)(2,1)S(1)}, bf16[2,4,16384]{2,1,0:T(4,128)(2,1)S(1)}, u32[]{:S(2)}, u32[]{:S(2)}) collective-permute-start(bf16[2,4,16384]{2,1,0:T(4,128)(2,1)S(1)} %get-tuple-element.567), channel_id=1, source_target_pairs={{0,12},{4,8},{8,4},{12,0},{1,13},{5,9},{9,5},{13,1},{2,14},{6,10},... | collective-permute-start | bytes 786440 | tf_op jit(solution)/shard_map/ppermute | solution.py:125
  125.7 1.8 collective-permute-start.7
  127.5 11.2 %collective-permute-start.8 = (f32[256,262]{1,0:T(8,128)S(1)}, f32[256,262]{1,0:T(8,128)S(1)}, u32[]{:S(2)}, u32[]{:S(2)}) collective-permute-start(f32[256,262]{1,0:T(8,128)S(1)} %fusion.186), channel_id=1, source_target_pairs={{0,2},{2,0},{1,3},{3,1},{4,6},{6,4},{5,7},{7,5},{8,10},{10,8},{9,1... | collective-permute-start | bytes 804872 | tf_op jit(solution)/shard_map/ppermute | solution.py:39
  138.8 13.4 %collective-permute-start.9 = (f32[256,262]{1,0:T(8,128)S(1)}, f32[256,262]{1,0:T(8,128)S(1)}, u32[]{:S(2)}, u32[]{:S(2)}) collective-permute-start(f32[256,262]{1,0:T(8,128)S(1)} %add.219), channel_id=1, source_target_pairs={{0,4},{4,0},{8,12},{12,8},{1,5},{5,1},{9,13},{13,9},{2,6},{6,2},{1... | collective-permute-start | bytes 804872 | tf_op jit(solution)/shard_map/ppermute | solution.py:39
  152.2 19.1 %collective-permute-start.10 = (f32[256,262]{1,0:T(8,128)S(1)}, f32[256,262]{1,0:T(8,128)S(1)}, u32[]{:S(2)}, u32[]{:S(2)}) collective-permute-start(f32[256,262]{1,0:T(8,128)S(1)} %add.220), channel_id=1, source_target_pairs={{0,8},{4,12},{8,0},{12,4},{1,9},{5,13},{9,1},{13,5},{2,10},{6,14},... | collective-permute-start | bytes 804872 | tf_op jit(solution)/shard_map/ppermute | solution.py:39
